TPU v7x, 512 devices: a whole 4x8x8 slice. The times are simulated.
512 devices in a mesh: grp: 16 (over z, core), dev: 32 (over x, y).
Axes of the slice: x: 4, y: 8, z: 8, core: 2. Of those that a mesh axis runs over, the one named last changes fastest.
Arguments:
- ssm_input: bfloat16 [4096, 4096], P('grp', 'dev'), may hold values from -6 to 6
- gate_input: bfloat16 [4096, 4096], P('grp', 'dev'), may hold values from -6 to 6
- step_size: float32 [4096, 64], P('grp', 'dev'), may hold values from 6.1035156e-05 to 0.3375
- decay_rate: float32 [64], P('dev'), may hold values from 0.5 to 2
- in_coeff: bfloat16 [4096, 128], P('grp'), may hold values from -6 to 6
- out_coeff: bfloat16 [4096, 128], P('grp'), may hold values from -6 to 6
- skip_gain: float32 [64], P('dev'), may hold values from 0.5 to 3
- norm_gain: float32 [4096], P('dev'), may hold values from 0.5 to 1.5
- out_proj: bfloat16 [4096, 2048], P(None, 'dev'), may hold values from -0.09375 to 0.09375
- residual: bfloat16 [4096, 2048], P(('grp', 'dev')), may hold values from -6 to 6
- ffn_gain: float32 [2048], replicated, may hold values from 0.5 to 1.5
- router: float32 [2048, 16], replicated, may hold values from -0.125 to 0.125
- routes: int32 [4096, 2], P(('grp', 'dev')), may hold values from 0 to 15, all different within a row; in each aligned block of 8 rows (0 to 7, 8 to 15, ...) at most 2 rows name the same one
- gate_weight: bfloat16 [16, 2048, 8192], P('grp', None, 'dev'), may hold values from -0.125 to 0.125
- up_weight: bfloat16 [16, 2048, 8192], P('grp', None, 'dev'), may hold values from -0.125 to 0.125
- down_weight: bfloat16 [16, 8192, 2048], P('grp', 'dev'), may hold values from -0.0625 to 0.0625
Outputs:
- moe_out: bfloat16 [4096, 2048], P(('grp', 'dev'))
Inputs may be any that keep to these rules, and one draw needn't show every extreme that they name: `routes`: each row names two different experts; among the 8 rows of one dispatch block of consecutive tokens no expert is named more than 2 times, a bound that some block reaches.
All inputs are finite; a program needn't handle non-finite values.
Results may differ from a plain program's by a relative error of at most 0.012.
Values may be sent and summed in bfloat16 or wider, within the bound.
No kernel may reach another device: no remote copies, remote signals or barrier semaphores. Data moves between devices by JAX's collectives and lax.ppermute only.
A program may use at most 64 MiB of HBM per device.

v0:
```python
import jax
import jax.numpy as jnp
from jax import lax
from jax.sharding import Mesh
from jax.sharding import PartitionSpec as P

DEV = ("dev_0", "dev_1")
GRP_DEV = ("grp", "dev_0", "dev_1")
EPSILON = 1e-05
HIGHEST_PREC = lax.Precision.HIGHEST


def side_by_side(arrays, axis, dim, along):
    columns = [a.reshape(*a.shape[:along], -1) for a in arrays]
    both = jnp.concatenate(columns, axis=along)
    filled, at, finished = (lax.all_gather(both, axis, axis=dim, tiled=True), 0, [])
    for a, column in zip(arrays, columns):
        piece = filled[..., at : at + column.shape[along]]
        finished.append(piece.reshape(*piece.shape[:along], *a.shape[along:]))
        at += column.shape[along]
    return tuple(finished)


def sent_to_all(shard, axis):
    peers = lax.axis_size(axis)
    return lax.all_to_all(
        jnp.broadcast_to(shard[None], (peers, *shard.shape)), axis, 0, 0, tiled=True
    )


def of_everyone(shard, axis):
    everything = sent_to_all(shard, axis)
    return jnp.sum(everything, axis=0)


def in_order(tiles, dim):
    dims = list(tiles.shape[1:])
    dims[dim] *= tiles.shape[0]
    return jnp.moveaxis(tiles, 0, dim).reshape(dims)


def collect(shard, axis, dim):
    return in_order(sent_to_all(shard, axis), dim)


def sum_by_axis(terms, axes):
    total = terms.astype(jnp.bfloat16)
    total = lax.psum_scatter(total, axes, scatter_dimension=0, tiled=True)
    return total.astype(jnp.float32)


def rms_scale(values, gain_vec):
    return (
        values * lax.rsqrt(jnp.mean(values * values, axis=-1, keepdims=True) + EPSILON) * gain_vec
    )


def slot_tables(routes_block, expert_count, slot_cap):
    blocks, row_total = (routes_block.shape[0], routes_block.shape[1])
    flat_routes = routes_block.reshape(blocks, row_total * 2)
    onehot = (
        flat_routes[:, :, None] == jnp.arange(expert_count, dtype=jnp.int32)[None, None, :]
    ).astype(jnp.int32)
    earlier = jnp.cumsum(onehot, axis=1) - onehot
    slot_rank = jnp.sum(earlier * onehot, axis=2)
    slot_index = (flat_routes * slot_cap + slot_rank).reshape(blocks, row_total, 2)
    placed = (
        slot_index[:, :, :, None]
        == jnp.arange(expert_count * slot_cap, dtype=jnp.int32)[None, None, None, :]
    )
    return placed.astype(jnp.float32)


def shards(
    ssm_input,
    gate_input,
    step_size,
    decay_rate,
    in_coeff,
    out_coeff,
    skip_gain,
    norm_gain,
    out_proj,
    residual,
    ffn_gain,
    router,
    routes,
    gate_weight,
    up_weight,
    down_weight,
):
    tok_rows = ssm_input.shape[0]
    head_count = step_size.shape[1]
    head_width = ssm_input.shape[1] // head_count
    dev_count = lax.axis_size(DEV)
    inner_dim = ssm_input.shape[1] * dev_count
    block_rows = residual.shape[0]
    model_dim = residual.shape[1]
    experts = lax.axis_size("grp")
    slot_cap = max(2, 4 * block_rows // experts)
    group_slots = experts * slot_cap
    inputs_f = ssm_input.astype(jnp.float32).reshape(tok_rows, head_count, head_width)
    in_float = in_coeff.astype(jnp.float32)
    out_float = out_coeff.astype(jnp.float32)
    log_rate = -(step_size * decay_rate[None, :])
    cumulative = jnp.cumsum(log_rate, axis=0)
    causal = (jnp.arange(tok_rows)[:, None] >= jnp.arange(tok_rows)[None, :])[:, :, None]
    spread = cumulative[:, None, :] - cumulative[None, :, :]
    decay_pair = jnp.where(causal, jnp.exp(jnp.where(causal, spread, 0.0)), 0.0)
    scores = jnp.dot(out_coeff, in_coeff.T, preferred_element_type=jnp.float32)
    mixing = decay_pair * scores[:, :, None] * step_size[None, :, :]
    inside = jnp.einsum("tuh,uhp->thp", mixing, inputs_f, precision=HIGHEST_PREC)
    to_end = jnp.exp(cumulative[-1][None, :] - cumulative) * step_size
    own_state = jnp.einsum("uh,uhp,un->hpn", to_end, inputs_f, in_float, precision=HIGHEST_PREC)
    own_log = cumulative[-1]
    group_logs, group_states = tuple(
        (
            part.astype(jnp.float32)
            for part in side_by_side(
                (own_log[None].astype(jnp.bfloat16), own_state[None].astype(jnp.bfloat16)),
                "grp",
                0,
                2,
            )
        )
    )
    group_index = jnp.arange(group_logs.shape[0])
    my_group = lax.axis_index("grp")
    inclusive = jnp.cumsum(group_logs, axis=0)
    exclusive = inclusive - group_logs
    before_me = jnp.sum(jnp.where((group_index == my_group)[:, None], exclusive, 0.0), axis=0)
    earlier_mask = (group_index < my_group)[:, None]
    weighting = jnp.where(
        earlier_mask, jnp.exp(jnp.where(earlier_mask, before_me[None, :] - inclusive, 0.0)), 0.0
    )
    entering = jnp.einsum("gh,ghpn->hpn", weighting, group_states, precision=HIGHEST_PREC)
    carried = jnp.exp(cumulative)[:, :, None] * jnp.einsum(
        "hpn,tn->thp", entering, out_float, precision=HIGHEST_PREC
    )
    ssm_out = inside + carried + skip_gain[None, :, None] * inputs_f
    gated_out = ssm_out.reshape(tok_rows, head_count * head_width) * jax.nn.silu(
        gate_input.astype(jnp.float32)
    )
    squares = lax.psum(jnp.sum(gated_out * gated_out, axis=1), DEV)
    mixed_rows = (
        gated_out * lax.rsqrt(squares[:, None] / inner_dim + EPSILON) * norm_gain[None, :]
    ).astype(jnp.bfloat16)
    gathered = lax.all_gather(mixed_rows, DEV, axis=0)
    projected = jnp.einsum(
        "dtc,dcf->tf",
        gathered,
        out_proj.reshape(dev_count, -1, out_proj.shape[1]),
        preferred_element_type=jnp.float32,
    ).astype(jnp.bfloat16)
    mamba_out = lax.all_to_all(projected, DEV, split_axis=0, concat_axis=1, tiled=True)
    hidden_res = (residual.astype(jnp.float32) + mamba_out.astype(jnp.float32)).astype(jnp.bfloat16)
    hidden_float = hidden_res.astype(jnp.float32)
    normed = rms_scale(hidden_float, ffn_gain).astype(jnp.bfloat16)
    logits = jnp.dot(normed.astype(jnp.float32), router, precision=HIGHEST_PREC)
    expert_ids = jnp.arange(experts, dtype=jnp.int32)[None, :]
    first_logit = jnp.sum(logits * (routes[:, 0:1] == expert_ids).astype(jnp.float32), axis=1)
    second_logit = jnp.sum(logits * (routes[:, 1:2] == expert_ids).astype(jnp.float32), axis=1)
    first_prob = jax.nn.sigmoid(first_logit - second_logit)
    second_prob = 1.0 - first_prob
    placed = slot_tables(routes[None], experts, slot_cap)[0]
    filled = jnp.sum(placed, axis=1)
    outgoing = jnp.dot(
        filled.T.astype(jnp.bfloat16), normed, preferred_element_type=jnp.float32
    ).astype(jnp.bfloat16)
    outgoing = outgoing.reshape(experts, slot_cap, model_dim)
    arrived = lax.all_to_all(outgoing, "grp", split_axis=0, concat_axis=0, tiled=True)
    all_rows = lax.all_gather(arrived, DEV, axis=0, tiled=True).reshape(-1, model_dim)
    gate_act = jnp.dot(all_rows, gate_weight[0], preferred_element_type=jnp.float32)
    up_act = jnp.dot(all_rows, up_weight[0], preferred_element_type=jnp.float32)
    hidden = (jax.nn.silu(gate_act) * up_act).astype(jnp.bfloat16)
    summed = sum_by_axis(jnp.dot(hidden, down_weight[0], preferred_element_type=jnp.float32), DEV)
    returned = lax.all_to_all(
        summed.astype(jnp.bfloat16).reshape(experts, slot_cap, model_dim),
        "grp",
        split_axis=0,
        concat_axis=0,
        tiled=True,
    )
    weights = first_prob[:, None] * placed[:, 0, :] + second_prob[:, None] * placed[:, 1, :]
    contrib = jnp.dot(
        weights,
        returned.reshape(group_slots, model_dim).astype(jnp.float32),
        precision=HIGHEST_PREC,
    )
    return (hidden_float + contrib).astype(jnp.bfloat16)


def solution(mesh):
    torus = Mesh(mesh.devices.reshape(mesh.shape["grp"], 4, 8), ("grp", "dev_0", "dev_1"))
    in_specs = (
        P("grp", DEV),
        P("grp", DEV),
        P("grp", DEV),
        P(DEV),
        P("grp", None),
        P("grp", None),
        P(DEV),
        P(DEV),
        P(None, DEV),
        P(GRP_DEV, None),
        P(),
        P(),
        P(GRP_DEV, None),
        P("grp", None, DEV),
        P("grp", None, DEV),
        P("grp", DEV, None),
    )
    out_specs = P(GRP_DEV, None)
    return jax.shard_map(
        shards, mesh=torus, in_specs=in_specs, out_specs=out_specs, check_vma=False
    )
```

profile of v0, /device:TPU:1, one launch (start us, length us, event | category | flops | bytes accessed | tf_op | source)
XLA Modules:
  0.0 574.6 jit_solution(1486846018110611630)
XLA Ops:
  6.6 0.9 negate_bitcast_fusion
  7.5 0.6 reduce-window.6
  8.1 0.2 slice_reduce_fusion
  8.3 0.2 reduce-window.9
  8.5 0.2 slice_reduce_fusion.1
  8.8 0.8 fusion.58
  9.5 0.9 copy.61
  10.5 1.0 convolution_convert_fusion.2
  11.6 0.1 pad_maximum_fusion
  11.7 26.0 %all_gather.12 = bf16[16,2,8193]{2,1,0:T(2,128)(2,1)S(1)} all-gather(bf16[1,2,8193]{2,1,0:T(2,128)(2,1)S(1)} %pad_maximum_fusion), channel_id=1, replica_groups=mesh['grp'=16,'dev_0'=4,'dev_1'=8] {'grp'}, dimensions={0}, use_global_device_ids=true | all-gather | bytes 557124 | tf_op jit(solution)/shard_map/all_gather | solution.py:16
  37.6 0.7 slice.40
  38.4 0.1 copy.76
  38.5 0.1 copy.64
  38.6 0.1 select_reduce_fusion.1
  38.8 0.1 copy.73
  38.9 0.4 reshape.234
  39.3 1.1 fusion.59
  40.3 0.6 fusion.18
  40.9 0.2 fusion.4
  41.2 0.6 fusion.3
  41.8 0.1 copy.66
  41.9 0.1 multiply_reduce_fusion
  42.0 61.3 %psum.7 = f32[256]{0:T(256)S(1)} all-reduce(f32[256]{0:T(256)S(1)} %multiply_reduce_fusion), channel_id=1, replica_groups=mesh['grp'=16,'dev_0'=4,'dev_1'=8] {'dev_0','dev_1'}, use_global_device_ids=true, to_apply=%region_5.6 | all-reduce | flops 256 | bytes 2048 | tf_op jit(solution)/shard_map/psum | solution.py:144
  103.4 0.7 multiply_convert_fusion
  104.4 0.2 select_reduce_fusion
  104.7 0.1 copy.72
  104.7 81.8 %all-gather.6.cloned.1.call-done = bf16[8192,128]{1,0:T(8,128)(2,1)} async-done(((bf16[256,128]{1,0:T(8,128)(2,1)}), bf16[8192,128]{1,0:T(8,128)(2,1)}) %all-gather.6.cloned.1.call-update) | async-done | bytes 2097168 | tf_op jit(solution)/shard_map/all_gather | solution.py:148
  186.6 2.3 fusion.5
  188.9 0.1 copy.68
  189.1 0.7 reshape.251
  189.8 4.9 all-to-all-start
  194.9 8.6 %all-to-all-done = bf16[32,2,256]{2,1,0:T(2,128)(2,1)S(1)} async-done(((bf16[32,2,256]{2,1,0:T(2,128)(2,1)}), bf16[32,2,256]{2,1,0:T(2,128)(2,1)S(1)}, u32[]{:S(2)}, u32[]{:S(2)}) %all-to-all-start) | async-done | bytes 32800 | tf_op jit(solution)/shard_map/all_to_all | solution.py:155
  203.5 0.1 reshape.252
  203.7 0.1 reshape.242
  203.8 0.1 fusion.37
  203.9 0.2 convolution_convert_fusion.1
  204.2 0.1 reshape.237
  204.3 22.8 %all_to_all.23 = bf16[16,2,2048]{2,1,0:T(2,128)(2,1)} all-to-all(bf16[16,2,2048]{2,1,0:T(2,128)(2,1)S(1)} %reshape.237), channel_id=1, replica_groups=mesh['grp'=16,'dev_0'=4,'dev_1'=8] {'grp'}, dimensions={0} | all-to-all | bytes 262144 | tf_op jit(solution)/shard_map/all_to_all | solution.py:171
  227.1 73.9 %all-gather.4.cloned.1.call-done = bf16[512,2,2048]{2,1,0:T(2,128)(2,1)} async-done(((bf16[16,2,2048]{2,1,0:T(2,128)(2,1)}), bf16[512,2,2048]{2,1,0:T(2,128)(2,1)}) %all-gather.4.cloned.1.call-update) | async-done | bytes 4194320 | tf_op jit(solution)/shard_map/all_gather | solution.py:172
  301.0 7.2 %reshape.238 = bf16[1024,2048]{1,0:T(8,128)(2,1)} reshape(bf16[512,2,2048]{2,1,0:T(2,128)(2,1)} %all-gather.4.cloned.1.call-done) | data formatting | bytes 8388608 | tf_op jit(solution)/shard_map/reshape | solution.py:172
  308.2 4.5 fusion.9
  312.8 9.1 %convolution_convert_fusion = bf16[1024,2048]{1,0:T(8,128)(2,1)} fusion(bf16[1024,2048]{1,0:T(8,128)(2,1)} %reshape.238, bf16[1,256,2048]{2,1,0:T(8,128)(2,1)S(1)} %copy-done, bf16[1,2048,256]{2,1,0:T(8,128)(2,1)} %param.30, f32[1024,256]{1,0:T(8,128)} %fusion.9), kind=kOutput, calls=%fused_computation | convolution fusion | flops 2151153664 | bytes 11534336 | tf_op jit(solution)/shard_map/dot_general | solution.py:176
  322.0 222.0 %reduce-scatter.2.cloned.1.call-done = bf16[32,2048]{1,0:T(8,128)(2,1)} async-done(((bf16[1024,2048]{1,0:T(8,128)(2,1)}), bf16[32,2048]{1,0:T(8,128)(2,1)}) %reduce-scatter.2.cloned.1.call-update) | async-done | bytes 131088 | tf_op jit(solution)/shard_map/reduce_scatter | solution.py:48
  544.0 1.7 reshape.239
  545.6 12.4 %all-to-all-start.2 = ((bf16[16,2,2048]{2,1,0:T(2,128)(2,1)}), bf16[16,2,2048]{2,1,0:T(2,128)(2,1)S(1)}, u32[]{:S(2)}, u32[]{:S(2)}) async-start(bf16[16,2,2048]{2,1,0:T(2,128)(2,1)} %reshape.239), calls=%async_computation.3 | async-start | bytes 262144 | tf_op jit(solution)/shard_map/all_to_all | solution.py:177
  558.0 0.3 select_reduce_fusion.2
  558.4 8.8 %all-to-all-done.2 = bf16[16,2,2048]{2,1,0:T(2,128)(2,1)S(1)} async-done(((bf16[16,2,2048]{2,1,0:T(2,128)(2,1)}), bf16[16,2,2048]{2,1,0:T(2,128)(2,1)S(1)}, u32[]{:S(2)}, u32[]{:S(2)}) %all-to-all-start.2) | async-done | bytes 131104 | tf_op jit(solution)/shard_map/all_to_all | solution.py:177
  567.2 0.9 fusion
  (56 shorter events, 1.2 us)
Async XLA Ops:
  6.5 306.2 %copy-start = (bf16[1,256,2048]{2,1,0:T(8,128)(2,1)S(1)}, bf16[1,256,2048]{2,1,0:T(8,128)(2,1)}, u32[]{:S(2)}) copy-start(bf16[1,256,2048]{2,1,0:T(8,128)(2,1)} %param.31) | copy-start | bytes 3145732
  6.5 34.6 %copy-start.6 = (f32[256,2]{0,1:T(2,128)S(1)}, f32[256,2]{0,1:T(2,128)}, u32[]{:S(2)}) copy-start(f32[256,2]{0,1:T(2,128)} %param.18) | copy-start | bytes 6148
  6.5 34.4 %copy-start.3 = (bf16[256,128]{1,0:T(8,128)(2,1)S(1)}, bf16[256,128]{1,0:T(8,128)(2,1)}, u32[]{:S(2)}) copy-start(bf16[256,128]{1,0:T(8,128)(2,1)} %param.21) | copy-start | bytes 196612
  6.5 34.6 %copy-start.11 = (f32[2]{0:T(128)S(1)}, f32[2]{0:T(128)}, u32[]{:S(2)}) copy-start(f32[2]{0:T(128)} %param.22) | copy-start | bytes 28
  6.5 35.3 %copy-start.2 = (bf16[256,128]{1,0:T(8,128)(2,1)S(1)}, bf16[256,128]{1,0:T(8,128)(2,1)}, u32[]{:S(2)}) copy-start(bf16[256,128]{1,0:T(8,128)(2,1)} %param.17) | copy-start | bytes 196612
  6.5 96.8 %copy-start.8 = (f32[128]{0:T(128)S(1)}, f32[128]{0:T(128)}, u32[]{:S(2)}) copy-start(f32[128]{0:T(128)} %param.23) | copy-start | bytes 1540
  6.6 97.5 %copy-start.7 = (s32[8,2]{0,1:T(2,128)S(1)}, s32[8,2]{0,1:T(2,128)}, u32[]{:S(2)}) copy-start(s32[8,2]{0,1:T(2,128)} %param.28) | copy-start | bytes 196
  6.6 180.0 %copy-start.1 = (bf16[4096,64]{0,1:T(8,128)(2,1)S(1)}, bf16[4096,64]{0,1:T(8,128)(2,1)}, u32[]{:S(2)}) copy-start(bf16[4096,64]{0,1:T(8,128)(2,1)} %param.24) | copy-start | bytes 1572868
  6.6 180.0 %all-gather.6.cloned.1.call-start = ((), (), s32[]{:S(2)}) async-start(), calls=%async_computation.6 | async-start | bytes 2162688 | tf_op jit(solution)/shard_map/all_gather | solution.py:148
  38.3 165.4 %copy-start.4 = (bf16[8,2048]{1,0:T(8,128)(2,1)S(1)}, bf16[8,2048]{1,0:T(8,128)(2,1)}, u32[]{:S(2)}) copy-start(bf16[8,2048]{1,0:T(8,128)(2,1)} %param.25) | copy-start | bytes 98308
  38.7 165.2 %copy-start.5 = (f32[2048]{0:T(1024)S(1)}, f32[2048]{0:T(1024)}, u32[]{:S(2)}) copy-start(f32[2048]{0:T(1024)} %param.26) | copy-start | bytes 24580
  189.8 13.7 %all-to-all-start = ((bf16[32,2,256]{2,1,0:T(2,128)(2,1)}), bf16[32,2,256]{2,1,0:T(2,128)(2,1)S(1)}, u32[]{:S(2)}, u32[]{:S(2)}) async-start(bf16[32,2,256]{2,1,0:T(2,128)(2,1)} %reshape.251), calls=%async_computation | async-start | bytes 65536 | tf_op jit(solution)/shard_map/all_to_all | solution.py:155
  194.7 106.3 %all-gather.4.cloned.1.call-start = ((), (), s32[]{:S(2)}) async-start(), calls=%async_computation.4 | async-start | bytes 4325376 | tf_op jit(solution)/shard_map/all_gather | solution.py:172
  227.1 81.2 %copy-start.9 = (bf16[1,2048,256]{2,1,0:T(8,128)(2,1)S(1)}, bf16[1,2048,256]{2,1,0:T(8,128)(2,1)}, u32[]{:S(2)}) copy-start(bf16[1,2048,256]{2,1,0:T(8,128)(2,1)} %param.29) | copy-start | bytes 3145732
  227.1 316.9 %reduce-scatter.2.cloned.1.call-start = ((), (), s32[]{:S(2)}) async-start(), calls=%async_computation.5 | async-start | bytes 4325376 | tf_op jit(solution)/shard_map/reduce_scatter | solution.py:48
  321.9 236.1 %copy-start.10 = (f32[2048,16]{0,1:T(8,128)S(1)}, f32[2048,16]{0,1:T(8,128)}, u32[]{:S(2)}) copy-start(f32[2048,16]{0,1:T(8,128)} %param.27) | copy-start | bytes 393220
  545.6 21.6 %all-to-all-start.2 = ((bf16[16,2,2048]{2,1,0:T(2,128)(2,1)}), bf16[16,2,2048]{2,1,0:T(2,128)(2,1)S(1)}, u32[]{:S(2)}, u32[]{:S(2)}) async-start(bf16[16,2,2048]{2,1,0:T(2,128)(2,1)} %reshape.239), calls=%async_computation.3 | async-start | bytes 262144 | tf_op jit(solution)/shard_map/all_to_all | solution.py:177
Sparse Core Ops, SparseCore 0:
  104.2 82.3 all-gather.5
  227.2 73.7 all-gather.3
  322.0 221.9 reduce-scatter.1
where the time goes:
time: 575 us
  waiting for transfers between devices  395 us (69%)
  blocking collectives  110 us (19%)
  matrix products  20.9 us (4%)
  starting transfers between devices  17.4 us (3%)
  between operations  13.4 us (2%)
  local copies, waits for them, and re-layouts  13.3 us (2%)
    reduce_scatter x1, waiting for transfers between devices, sum_by_axis(): total = lax.psum_scatter(total, axes, scatter_dimension=0, tiled=True)  222 us
    all_gather x1, waiting for transfers between devices, shards(): gathered = lax.all_gather(mixed_rows, DEV, axis=0)  81.8 us
    all_gather x1, waiting for transfers between devices, shards(): lax.all_gather(arrived, DEV, axis=0, tiled=True).reshape(-1, model_dim)  73.9 us
    psum x1, blocking collectives, shards(): squares = lax.psum(jnp.sum(gated_out * gated_out, axis=1), DEV)  61.3 us
    all_gather x1, blocking collectives, side_by_side(): lax.all_gather(both, axis, axis=dim, tiled=True)  26 us
    all_to_all x1, blocking collectives, shards(): lax.all_to_all(outgoing, 'grp', split_axis=0, concat_axis=0, tiled=True)  22.8 us
    all_to_all x1, starting transfers between devices, shards(): lax.all_to_all(summed.astype(jnp.bfloat16).reshape(experts, slot_cap, mod...  12.4 us
  transfers between devices with their start and end apart: 5, of which 5 were waited for; matrix products, arithmetic and copies ran while one was open for 0% of the time, Pallas kernels for 0%

commit v1 on v0

--- a/solution.py
+++ b/solution.py
@@ -89,6 +89,11 @@
     up_weight,
     down_weight,
 ):
+
+    def _cut_rails(panel):
+        formed = lax.all_gather(panel, DEV).sum(axis=0)
+        return formed
+
     tok_rows = ssm_input.shape[0]
     head_count = step_size.shape[1]
     head_width = ssm_input.shape[1] // head_count
@@ -141,7 +146,7 @@
     gated_out = ssm_out.reshape(tok_rows, head_count * head_width) * jax.nn.silu(
         gate_input.astype(jnp.float32)
     )
-    squares = lax.psum(jnp.sum(gated_out * gated_out, axis=1), DEV)
+    squares = _cut_rails(jnp.sum(gated_out * gated_out, axis=1))
     mixed_rows = (
         gated_out * lax.rsqrt(squares[:, None] / inner_dim + EPSILON) * norm_gain[None, :]
     ).astype(jnp.bfloat16)

time: 575 us -> 544 us (0.946)
  blocking collectives: 110 us -> 79.6 us
    psum x1 -> x0, blocking collectives: 61.3 us -> none  [shards(): squares = lax.psum(jnp.sum(gated_out * gated_out, axis=1), DEV)]
    all_gather x0 -> x1, blocking collectives: none -> 30.9 us  [_cut_rails(): formed = lax.all_gather(panel, DEV).sum(axis=0)]
where the time goes in v1:
time: 544 us; the launch traced here: 543 us
  waiting for transfers between devices  394 us (72%)
  blocking collectives  79.6 us (15%)
  matrix products  20.9 us (4%)
  starting transfers between devices  17.9 us (3%)
  between operations  13.4 us (2%)
  local copies, waits for them, and re-layouts  13.3 us (2%)
    reduce_scatter x1, waiting for transfers between devices, sum_by_axis(): total = lax.psum_scatter(total, axes, scatter_dimension=0, tiled=True)  221 us
    all_gather x1, waiting for transfers between devices, shards(): gathered = lax.all_gather(mixed_rows, DEV, axis=0)  80.8 us
    all_gather x1, waiting for transfers between devices, shards(): lax.all_gather(arrived, DEV, axis=0, tiled=True).reshape(-1, model_dim)  73.9 us
    all_gather x1, blocking collectives, _cut_rails(): formed = lax.all_gather(panel, DEV).sum(axis=0)  30.9 us
    all_gather x1, blocking collectives, side_by_side(): lax.all_gather(both, axis, axis=dim, tiled=True)  26 us
    all_to_all x1, blocking collectives, shards(): lax.all_to_all(outgoing, 'grp', split_axis=0, concat_axis=0, tiled=True)  22.8 us
    all_to_all x1, starting transfers between devices, shards(): lax.all_to_all(summed.astype(jnp.bfloat16).reshape(experts, slot_cap, mod...  12.8 us
  transfers between devices with their start and end apart: 5, of which 5 were waited for; matrix products, arithmetic and copies ran while one was open for 0% of the time, Pallas kernels for 0%

profile of v1, /device:TPU:1, one launch (start us, length us, event | category | flops | bytes accessed | tf_op | source)
XLA Modules:
  0.0 543.1 jit_solution(7835378679500422201)
XLA Ops:
  6.6 0.9 negate_bitcast_fusion
  7.5 0.6 reduce-window.6
  8.1 0.2 slice_reduce_fusion
  8.3 0.2 reduce-window.9
  8.5 0.2 slice_reduce_fusion.1
  8.8 0.8 fusion.58
  9.5 0.9 copy.61
  10.5 1.0 convolution_convert_fusion.2
  11.6 0.1 pad_maximum_fusion
  11.7 26.0 %all_gather.18 = bf16[16,2,8193]{2,1,0:T(2,128)(2,1)S(1)} all-gather(bf16[1,2,8193]{2,1,0:T(2,128)(2,1)S(1)} %pad_maximum_fusion), channel_id=1, replica_groups=mesh['grp'=16,'dev_0'=4,'dev_1'=8] {'grp'}, dimensions={0}, use_global_device_ids=true | all-gather | bytes 557124 | tf_op jit(solution)/shard_map/all_gather | solution.py:16
  37.6 0.7 slice.40
  38.4 0.1 copy.76
  38.5 0.1 copy.64
  38.6 0.1 select_reduce_fusion.1
  38.8 0.1 copy.73
  38.9 0.4 reshape.238
  39.3 1.1 fusion.59
  40.3 0.6 fusion.18
  40.9 0.2 fusion.4
  41.2 0.6 fusion.3
  41.8 0.1 copy.66
  41.9 0.1 multiply_reduce_fusion
  42.0 30.9 %all-gather.2 = f32[32,1,256]{2,1,0:T(1,128)S(1)} all-gather(f32[1,1,256]{2,1,0:T(1,128)S(1)} %bitcast.96), channel_id=2, replica_groups=mesh['grp'=16,'dev_0'=4,'dev_1'=8] {'dev_0','dev_1'}, dimensions={0}, use_global_device_ids=true | all-gather | bytes 33792 | tf_op jit(solution)/shard_map/all_gather | solution.py:94
  73.0 0.7 multiply_convert_fusion
  74.1 0.2 select_reduce_fusion
  74.3 0.1 copy.72
  74.4 80.8 %all-gather.8.cloned.1.call-done = bf16[8192,128]{1,0:T(8,128)(2,1)} async-done(((bf16[256,128]{1,0:T(8,128)(2,1)}), bf16[8192,128]{1,0:T(8,128)(2,1)}) %all-gather.8.cloned.1.call-update) | async-done | bytes 2097168 | tf_op jit(solution)/shard_map/all_gather | solution.py:153
  155.2 2.3 fusion.5
  157.5 0.1 copy.68
  157.6 0.7 reshape.259
  158.4 4.9 all-to-all-start
  163.5 8.6 %all-to-all-done = bf16[32,2,256]{2,1,0:T(2,128)(2,1)S(1)} async-done(((bf16[32,2,256]{2,1,0:T(2,128)(2,1)}), bf16[32,2,256]{2,1,0:T(2,128)(2,1)S(1)}, u32[]{:S(2)}, u32[]{:S(2)}) %all-to-all-start) | async-done | bytes 32800 | tf_op jit(solution)/shard_map/all_to_all | solution.py:160
  172.1 0.1 reshape.260
  172.3 0.1 reshape.246
  172.4 0.1 fusion.37
  172.5 0.2 convolution_convert_fusion.1
  172.8 0.1 reshape.241
  172.9 22.8 %all_to_all.23 = bf16[16,2,2048]{2,1,0:T(2,128)(2,1)} all-to-all(bf16[16,2,2048]{2,1,0:T(2,128)(2,1)S(1)} %reshape.241), channel_id=1, replica_groups=mesh['grp'=16,'dev_0'=4,'dev_1'=8] {'grp'}, dimensions={0} | all-to-all | bytes 262144 | tf_op jit(solution)/shard_map/all_to_all | solution.py:176
  195.7 73.9 %all-gather.6.cloned.1.call-done = bf16[512,2,2048]{2,1,0:T(2,128)(2,1)} async-done(((bf16[16,2,2048]{2,1,0:T(2,128)(2,1)}), bf16[512,2,2048]{2,1,0:T(2,128)(2,1)}) %all-gather.6.cloned.1.call-update) | async-done | bytes 4194320 | tf_op jit(solution)/shard_map/all_gather | solution.py:177
  269.6 7.2 %reshape.242 = bf16[1024,2048]{1,0:T(8,128)(2,1)} reshape(bf16[512,2,2048]{2,1,0:T(2,128)(2,1)} %all-gather.6.cloned.1.call-done) | data formatting | bytes 8388608 | tf_op jit(solution)/shard_map/reshape | solution.py:177
  276.8 4.5 fusion.9
  281.3 9.1 %convolution_convert_fusion = bf16[1024,2048]{1,0:T(8,128)(2,1)} fusion(bf16[1024,2048]{1,0:T(8,128)(2,1)} %reshape.242, bf16[1,256,2048]{2,1,0:T(8,128)(2,1)S(1)} %copy-done, bf16[1,2048,256]{2,1,0:T(8,128)(2,1)} %param.30, f32[1024,256]{1,0:T(8,128)} %fusion.9), kind=kOutput, calls=%fused_computation | convolution fusion | flops 2151153664 | bytes 11534336 | tf_op jit(solution)/shard_map/dot_general | solution.py:181
  290.6 221.4 %reduce-scatter.2.cloned.1.call-done = bf16[32,2048]{1,0:T(8,128)(2,1)} async-done(((bf16[1024,2048]{1,0:T(8,128)(2,1)}), bf16[32,2048]{1,0:T(8,128)(2,1)}) %reduce-scatter.2.cloned.1.call-update) | async-done | bytes 131088 | tf_op jit(solution)/shard_map/reduce_scatter | solution.py:48
  512.0 1.7 reshape.243
  513.6 12.8 %all-to-all-start.2 = ((bf16[16,2,2048]{2,1,0:T(2,128)(2,1)}), bf16[16,2,2048]{2,1,0:T(2,128)(2,1)S(1)}, u32[]{:S(2)}, u32[]{:S(2)}) async-start(bf16[16,2,2048]{2,1,0:T(2,128)(2,1)} %reshape.243), calls=%async_computation.3 | async-start | bytes 262144 | tf_op jit(solution)/shard_map/all_to_all | solution.py:182
  526.5 0.3 select_reduce_fusion.2
  526.8 8.8 %all-to-all-done.2 = bf16[16,2,2048]{2,1,0:T(2,128)(2,1)S(1)} async-done(((bf16[16,2,2048]{2,1,0:T(2,128)(2,1)}), bf16[16,2,2048]{2,1,0:T(2,128)(2,1)S(1)}, u32[]{:S(2)}, u32[]{:S(2)}) %all-to-all-start.2) | async-done | bytes 131104 | tf_op jit(solution)/shard_map/all_to_all | solution.py:182
  535.7 0.9 fusion
  (57 shorter events, 1.3 us)
Async XLA Ops:
  6.5 274.8 %copy-start = (bf16[1,256,2048]{2,1,0:T(8,128)(2,1)S(1)}, bf16[1,256,2048]{2,1,0:T(8,128)(2,1)}, u32[]{:S(2)}) copy-start(bf16[1,256,2048]{2,1,0:T(8,128)(2,1)} %param.31) | copy-start | bytes 3145732
  6.5 34.6 %copy-start.6 = (f32[256,2]{0,1:T(2,128)S(1)}, f32[256,2]{0,1:T(2,128)}, u32[]{:S(2)}) copy-start(f32[256,2]{0,1:T(2,128)} %param.18) | copy-start | bytes 6148
  6.5 34.4 %copy-start.3 = (bf16[256,128]{1,0:T(8,128)(2,1)S(1)}, bf16[256,128]{1,0:T(8,128)(2,1)}, u32[]{:S(2)}) copy-start(bf16[256,128]{1,0:T(8,128)(2,1)} %param.21) | copy-start | bytes 196612
  6.5 34.6 %copy-start.11 = (f32[2]{0:T(128)S(1)}, f32[2]{0:T(128)}, u32[]{:S(2)}) copy-start(f32[2]{0:T(128)} %param.22) | copy-start | bytes 28
  6.5 35.3 %copy-start.2 = (bf16[256,128]{1,0:T(8,128)(2,1)S(1)}, bf16[256,128]{1,0:T(8,128)(2,1)}, u32[]{:S(2)}) copy-start(bf16[256,128]{1,0:T(8,128)(2,1)} %param.17) | copy-start | bytes 196612
  6.5 66.5 %copy-start.8 = (f32[128]{0:T(128)S(1)}, f32[128]{0:T(128)}, u32[]{:S(2)}) copy-start(f32[128]{0:T(128)} %param.23) | copy-start | bytes 1540
  6.6 67.2 %copy-start.7 = (s32[8,2]{0,1:T(2,128)S(1)}, s32[8,2]{0,1:T(2,128)}, u32[]{:S(2)}) copy-start(s32[8,2]{0,1:T(2,128)} %param.28) | copy-start | bytes 196
  6.6 148.6 %copy-start.1 = (bf16[4096,64]{0,1:T(8,128)(2,1)S(1)}, bf16[4096,64]{0,1:T(8,128)(2,1)}, u32[]{:S(2)}) copy-start(bf16[4096,64]{0,1:T(8,128)(2,1)} %param.24) | copy-start | bytes 1572868
  6.6 148.6 %all-gather.8.cloned.1.call-start = ((), (), s32[]{:S(2)}) async-start(), calls=%async_computation.6 | async-start | bytes 2162688 | tf_op jit(solution)/shard_map/all_gather | solution.py:153
  38.4 134.0 %copy-start.4 = (bf16[8,2048]{1,0:T(8,128)(2,1)S(1)}, bf16[8,2048]{1,0:T(8,128)(2,1)}, u32[]{:S(2)}) copy-start(bf16[8,2048]{1,0:T(8,128)(2,1)} %param.25) | copy-start | bytes 98308
  38.9 133.6 %copy-start.5 = (f32[2048]{0:T(1024)S(1)}, f32[2048]{0:T(1024)}, u32[]{:S(2)}) copy-start(f32[2048]{0:T(1024)} %param.26) | copy-start | bytes 24580
  158.4 13.7 %all-to-all-start = ((bf16[32,2,256]{2,1,0:T(2,128)(2,1)}), bf16[32,2,256]{2,1,0:T(2,128)(2,1)S(1)}, u32[]{:S(2)}, u32[]{:S(2)}) async-start(bf16[32,2,256]{2,1,0:T(2,128)(2,1)} %reshape.259), calls=%async_computation | async-start | bytes 65536 | tf_op jit(solution)/shard_map/all_to_all | solution.py:160
  163.3 106.3 %all-gather.6.cloned.1.call-start = ((), (), s32[]{:S(2)}) async-start(), calls=%async_computation.4 | async-start | bytes 4325376 | tf_op jit(solution)/shard_map/all_gather | solution.py:177
  195.7 81.2 %copy-start.9 = (bf16[1,2048,256]{2,1,0:T(8,128)(2,1)S(1)}, bf16[1,2048,256]{2,1,0:T(8,128)(2,1)}, u32[]{:S(2)}) copy-start(bf16[1,2048,256]{2,1,0:T(8,128)(2,1)} %param.29) | copy-start | bytes 3145732
  195.7 316.3 %reduce-scatter.2.cloned.1.call-start = ((), (), s32[]{:S(2)}) async-start(), calls=%async_computation.5 | async-start | bytes 4325376 | tf_op jit(solution)/shard_map/reduce_scatter | solution.py:48
  290.4 236.0 %copy-start.10 = (f32[2048,16]{0,1:T(8,128)S(1)}, f32[2048,16]{0,1:T(8,128)}, u32[]{:S(2)}) copy-start(f32[2048,16]{0,1:T(8,128)} %param.27) | copy-start | bytes 393220
  513.6 22.0 %all-to-all-start.2 = ((bf16[16,2,2048]{2,1,0:T(2,128)(2,1)}), bf16[16,2,2048]{2,1,0:T(2,128)(2,1)S(1)}, u32[]{:S(2)}, u32[]{:S(2)}) async-start(bf16[16,2,2048]{2,1,0:T(2,128)(2,1)} %reshape.243), calls=%async_computation.3 | async-start | bytes 262144 | tf_op jit(solution)/shard_map/all_to_all | solution.py:182
Sparse Core Ops, SparseCore 0:
  73.9 81.2 all-gather.7
  195.8 73.7 all-gather.5
  290.6 221.3 reduce-scatter.1
